TPU v7x, 32 devices: a whole 2x2x4 slice. The times are simulated.
32 devices in a mesh: dp: 4 (over x, core), pipe: 2 (over y), tensor: 4 (over z).
Axes of the slice: x: 2, y: 2, z: 4, core: 2. Of those that a mesh axis runs over, the one named last changes fastest.
Arguments:
- layer_input: bfloat16 [4, 2, 512, 8192], P('dp', 'pipe', None, 'tensor'), may hold values from -40 to 40
- output_grad: bfloat16 [4, 2, 512, 8192], P('dp', 'pipe', None, 'tensor'), may hold values from -6 to 6
- kv_grad: bfloat16 [4, 2, 512, 2048], P('dp', 'pipe', None, 'tensor'), may hold values from -6 to 6
- norm_gain: bfloat16 [2, 8192], P('pipe', 'tensor'), may hold values from 0.5 to 1.5
- kv_weight: bfloat16 [2, 8192, 2048], P('pipe', 'tensor'), may hold values from -0.0625 to 0.0625
Outputs:
- upstream_grad: bfloat16 [4, 2, 512, 8192], P('dp', 'pipe', None, 'tensor')
- kv_weight_grad: bfloat16 [2, 8192, 2048], P('pipe', 'tensor', 'dp')
- gain_grad: float32 [2, 8192], P('pipe', 'tensor')
All inputs are finite; a program needn't handle non-finite values.
Results may differ from a plain program's by a relative error of at most 0.009.
Values may be sent and summed in bfloat16 or wider, within the bound.
No kernel may reach another device: no remote copies, remote signals or barrier semaphores. Data moves between devices by JAX's collectives and lax.ppermute only.
A program may use at most 128 MiB of HBM per device.

v0:
```python
import jax
import jax.numpy as jnp
from jax import lax
from jax.sharding import PartitionSpec as P

D = 8192


def from_behind(block, axis, distance):
    devices = range(lax.axis_size(axis))
    route = [(i - distance, i) for i in devices if i - distance in devices]
    return lax.ppermute(block, axis, route)


def on_device(layer_input, output_grad, kv_grad, norm_gain, kv_weight):
    rows = layer_input[0, 0]
    grad_out = output_grad[0, 0]
    grad_kv = kv_grad[0, 0]
    gain_f = norm_gain[0].astype(jnp.float32)
    weight = kv_weight[0]
    values = rows.astype(jnp.float32)
    local_squares = jnp.sum(values * values, axis=1, keepdims=True)
    total_squares = lax.psum(local_squares, "tensor")
    rstd = lax.rsqrt(total_squares / D + 1e-05)
    normed = values * rstd
    hidden = (normed * gain_f).astype(jnp.bfloat16)
    piece = lax.all_gather(grad_kv, "tensor", axis=1, tiled=True)
    row_total = lax.dot_general(
        piece, weight, (((1,), (1,)), ((), ())), preferred_element_type=jnp.float32
    )
    term = lax.dot_general(
        hidden, piece, (((0,), (0,)), ((), ())), preferred_element_type=jnp.float32
    )
    weight_total = term
    wgrad = weight_total
    scaled = gain_f * row_total
    local_dot = jnp.sum(scaled * normed, axis=1, keepdims=True)
    mean_term = lax.psum(local_dot, "tensor") / D
    input_grad = (grad_out.astype(jnp.float32) + rstd * (scaled - normed * mean_term)).astype(
        jnp.bfloat16
    )
    upstream = from_behind(input_grad, "pipe", -1)
    gain_part = jnp.sum(row_total * normed, axis=0)
    gain_total = lax.psum(gain_part, "dp")
    weight_total = lax.psum_scatter(
        wgrad.astype(jnp.bfloat16), "dp", scatter_dimension=1, tiled=True
    )
    return (upstream[None, None], weight_total[None], gain_total[None])


def solution(mesh):
    in_specs = (
        P("dp", "pipe", None, "tensor"),
        P("dp", "pipe", None, "tensor"),
        P("dp", "pipe", None, "tensor"),
        P("pipe", "tensor"),
        P("pipe", "tensor", None),
    )
    out_specs = (P("dp", "pipe", None, "tensor"), P("pipe", "tensor", "dp"), P("pipe", "tensor"))
    return jax.shard_map(
        on_device, mesh=mesh, in_specs=in_specs, out_specs=out_specs, check_vma=False
    )
```

profile of v0, /device:TPU:0, one launch (start us, length us, event | category | flops | bytes accessed | tf_op | source)
XLA Modules:
  0.0 152.9 jit_solution(5806783644709270451)
XLA Ops:
  7.2 0.0 all-gather.3.cloned.1.call-start
  7.2 0.7 all-gather.3.cloned.1.call-update
  7.9 0.0 reduce-scatter.2.cloned.1.call-start
  7.9 0.7 mul.69
  8.7 2.1 %fusion.13 = f32[512]{0:T(512)S(1)} fusion(bf16[1,1,512,2048]{3,2,1,0:T(8,128)(2,1)} %param.5), kind=kLoop, calls=%fused_computation.16 | loop fusion | flops 3145216 | bytes 2099200 | tf_op jit(solution)/shard_map/reduce_sum | solution.py:22
  10.7 13.7 %psum.21 = f32[512,1]{0,1:T(1,128)S(1)} all-reduce(f32[512,1]{0,1:T(1,128)S(1)} %bitcast.37), channel_id=1, replica_groups=mesh['dp'=4,'pipe'=2,'tensor'=4] {'tensor'}, use_global_device_ids=true, to_apply=%region_1.0 | all-reduce | flops 512 | bytes 4096 | tf_op jit(solution)/shard_map/psum | solution.py:23
  24.4 33.9 %all-gather.3.cloned.1.call-done = bf16[1,1,512,2048]{3,2,1,0:T(8,128)(2,1)} async-done(((bf16[1,1,512,512]{3,2,1,0:T(8,128)(2,1)}), bf16[1,1,512,2048]{3,2,1,0:T(8,128)(2,1)}) %all-gather.3.cloned.1.call-update) | async-done | bytes 2097168 | tf_op jit(solution)/shard_map/all_gather | solution.py:27
  58.3 10.1 %convolution_convert_fusion = bf16[2048,2048]{1,0:T(8,128)(2,1)} fusion(bf16[1,1,512,2048]{3,2,1,0:T(8,128)(2,1)} %param.5, bf16[1,1,512,2048]{3,2,1,0:T(8,128)(2,1)} %all-gather.3.cloned.1.call-done, f32[2048]{0:T(1024)S(1)} %bitcast.34, f32[512]{0:T(512)S(1)} %bitcast.39), kind=kOutput, calls=%fused_computation.2 | convolution fusion | flops 4303355904 | bytes 12593152 | tf_op jit(solution)/shard_map/dot_general | solution.py:31
  68.4 0.0 copy-start
  68.4 0.0 reduce-scatter.2.cloned.1.call-update
  68.4 1.6 %copy-done = bf16[1,1,512,2048]{3,2,1,0:T(8,128)(2,1)S(1)} copy-done((bf16[1,1,512,2048]{3,2,1,0:T(8,128)(2,1)S(1)}, bf16[1,1,512,2048]{3,2,1,0:T(8,128)(2,1)}, u32[]{:S(2)}) %copy-start) | copy-done | bytes 2097176
  70.0 11.8 %fusion.12 = (f32[2048]{0:T(1024)S(1)}, f32[512]{0:T(512)S(1)}, f32[512,2048]{1,0:T(8,128)}) fusion(bf16[1,1,512,2048]{3,2,1,0:T(8,128)(2,1)S(1)} %copy-done, f32[512]{0:T(512)S(1)} %bitcast.40, f32[2048]{0:T(1024)S(1)} %bitcast.35, bf16[1,2048,2048]{2,1,0:T(8,128)(2,1)} %param.9, bf16[1,1,512,2048]{3,2,1,0:T(8,128)(2,1)} %all-gather.3.cloned.1.call-done), kind=kOutput, calls=%fused_computation.15 | convolution fusion | flops 4302304768 | bytes 16797696 | tf_op jit(solution)/shard_map/dot_general | solution.py:28
  81.8 9.0 %psum.22 = f32[512,1]{0,1:T(1,128)S(1)} all-reduce(f32[512,1]{0,1:T(1,128)S(1)} %bitcast.43), channel_id=1, replica_groups=mesh['dp'=4,'pipe'=2,'tensor'=4] {'tensor'}, use_global_device_ids=true, to_apply=%region_3.0 | all-reduce | flops 512 | bytes 4096 | tf_op jit(solution)/shard_map/psum | solution.py:38
  90.8 5.7 %fusion.10 = bf16[512,2048]{1,0:T(8,128)(2,1)} fusion(f32[512,2048]{1,0:T(8,128)} %get-tuple-element.5, bf16[1,1,512,2048]{3,2,1,0:T(8,128)(2,1)} %param.6, bf16[1,1,512,2048]{3,2,1,0:T(8,128)(2,1)S(1)} %copy-done, f32[512]{0:T(512)S(1)} %bitcast.42, f32[2048]{0:T(1024)S(1)} %bitcast.36, f32[512]{0:T(512)S(1)} %bitcast.41), kind=kLoop, calls=%fused_computation.13 | loop fusion | flops 9437184 | bytes 10498048 | tf_op jit(solution)/shard_map/convert_element_type | solution.py:39
  96.5 1.3 collective-permute-start
  97.8 7.0 %psum.23 = f32[1,2048]{1,0:T(1,128)} all-reduce(f32[1,2048]{1,0:T(1,128)S(1)} %bitcast.38), channel_id=1, replica_groups=mesh['dp'=4,'pipe'=2,'tensor'=4] {'dp'}, use_global_device_ids=true, to_apply=%region_6.0 | all-reduce | flops 2048 | bytes 16384 | tf_op jit(solution)/shard_map/psum | solution.py:44
  104.8 39.9 %collective-permute-done = bf16[512,2048]{1,0:T(8,128)(2,1)S(1)} collective-permute-done((bf16[512,2048]{1,0:T(8,128)(2,1)}, bf16[512,2048]{1,0:T(8,128)(2,1)S(1)}, u32[]{:S(2)}, u32[]{:S(2)}) %collective-permute-start) | collective-permute-done | bytes 2097184 | tf_op jit(solution)/shard_map/ppermute | solution.py:12
  144.7 0.0 reduce-scatter.2.cloned.1.call-done
  144.7 1.3 copy.9
  (2 shorter events, 0.0 us)
Async XLA Ops:
  7.2 51.1 %all-gather.3.cloned.1.call-start = ((), (), s32[]{:S(2)}) async-start(), calls=%async_computation.2 | async-start | bytes 2621440 | tf_op jit(solution)/shard_map/all_gather | solution.py:27
  7.9 136.8 %reduce-scatter.2.cloned.1.call-start = ((), (), s32[]{:S(2)}) async-start(), calls=%async_computation.1 | async-start | bytes 10485760 | tf_op jit(solution)/shard_map/reduce_scatter | solution.py:45
  68.4 1.6 %copy-start = (bf16[1,1,512,2048]{3,2,1,0:T(8,128)(2,1)S(1)}, bf16[1,1,512,2048]{3,2,1,0:T(8,128)(2,1)}, u32[]{:S(2)}) copy-start(bf16[1,1,512,2048]{3,2,1,0:T(8,128)(2,1)} %param.5) | copy-start | bytes 6291460
  96.5 48.2 %collective-permute-start = (bf16[512,2048]{1,0:T(8,128)(2,1)}, bf16[512,2048]{1,0:T(8,128)(2,1)S(1)}, u32[]{:S(2)}, u32[]{:S(2)}) collective-permute-start(bf16[512,2048]{1,0:T(8,128)(2,1)} %fusion.10), channel_id=1, source_target_pairs={{4,0},{5,1},{6,2},{7,3},{12,8},{13,9},{14,10},{15,11},{20,16},{21,... | collective-permute-start | bytes 6291464 | tf_op jit(solution)/shard_map/ppermute | solution.py:12
Sparse Core Ops, SparseCore 0:
  9.6 48.6 all-gather.2
  68.5 70.6 reduce-scatter.1
where the time goes:
time: 153 us
  waiting for transfers between devices  74.5 us (49%)
  blocking collectives  29.6 us (19%)
  matrix products  21.9 us (14%)
  between operations  14.1 us (9%)
  other arithmetic  8.53 us (6%)
  local copies, waits for them, and re-layouts  2.89 us (2%)
    ppermute x1, waiting for transfers between devices, from_behind(): return lax.ppermute(block, axis, route)  39.9 us
    all_gather x1, waiting for transfers between devices, on_device(): piece = lax.all_gather(grad_kv, 'tensor', axis=1, tiled=True)  33.9 us
    psum x1, blocking collectives, on_device(): total_squares = lax.psum(local_squares, 'tensor')  13.7 us
    dot_general x1, matrix products, on_device(): lax.dot_general(piece, weight, (((1,), (1,)), ((), ())), preferred_elemen...  11.8 us
    dot_general x1, matrix products, on_device(): lax.dot_general(hidden, piece, (((0,), (0,)), ((), ())), preferred_elemen...  10.1 us
    psum x1, blocking collectives, on_device(): mean_term = lax.psum(local_dot, 'tensor') / D  8.96 us
    psum x1, blocking collectives, on_device(): gain_total = lax.psum(gain_part, 'dp')  7.03 us
    convert_element_type x1, other arithmetic, on_device(): (grad_out.astype(jnp.float32) + rstd * (scaled - normed * mean_term)).ast...  5.73 us
  transfers between devices with their start and end apart: 3, of which 2 were waited for; matrix products, arithmetic and copies ran while one was open for 13% of the time, Pallas kernels for 0%

commit v1 on v0

--- a/solution.py
+++ b/solution.py
@@ -4,6 +4,18 @@
 from jax.sharding import PartitionSpec as P
 
 D = 8192
+
+
+def gather_by_bits(x, axis, dim):
+    ways, here, step = (lax.axis_size(axis), lax.axis_index(axis), x.shape[dim])
+    line, have = (x, 1)
+    while have < ways:
+        line = jnp.concatenate(
+            [line, lax.ppermute(line, axis, [(d, (d - have) % ways) for d in range(ways)])],
+            axis=dim,
+        )
+        have = 2 * have
+    return jnp.roll(line, here * step, axis=dim)
 
 
 def from_behind(block, axis, distance):
@@ -24,7 +36,7 @@
     rstd = lax.rsqrt(total_squares / D + 1e-05)
     normed = values * rstd
     hidden = (normed * gain_f).astype(jnp.bfloat16)
-    piece = lax.all_gather(grad_kv, "tensor", axis=1, tiled=True)
+    piece = gather_by_bits(grad_kv, "tensor", 1)
     row_total = lax.dot_general(
         piece, weight, (((1,), (1,)), ((), ())), preferred_element_type=jnp.float32
     )

time: 153 us -> 170 us (1.11)
  blocking collectives: 29.6 us -> 45.3 us
  waiting for transfers between devices: 74.5 us -> 66.9 us
  starting transfers between devices: 1.36 us -> 7.78 us
  matrix products: 21.9 us -> 18.3 us
  local copies, waits for them, and re-layouts: 2.89 us -> 6.15 us
  other arithmetic: 8.53 us -> 11.3 us
    all_gather x1 -> x0, waiting for transfers between devices: 33.9 us -> none  [on_device(): piece = lax.all_gather(grad_kv, 'tensor', axis=1, tiled=True)]
    ppermute x0 -> x2, waiting for transfers between devices: none -> 29.9 us  [gather_by_bits(): lax.ppermute(line, axis, [(d, (d - have) % ways) for d in range(ways)])]
    psum x1, blocking collectives: 13.7 us -> 25.2 us  [on_device(): total_squares = lax.psum(local_squares, 'tensor')]
    ppermute x0 -> x2, starting transfers between devices: none -> 6.47 us  [gather_by_bits(): lax.ppermute(line, axis, [(d, (d - have) % ways) for d in range(ways)])]
    psum x1, blocking collectives: 8.96 us -> 13.1 us  [on_device(): mean_term = lax.psum(local_dot, 'tensor') / D]
    dot_general x1, matrix products: 10.1 us -> 7.1 us  [on_device(): lax.dot_general(hidden, piece, (((0,), (0,)), ((), ())), preferred_elemen...]
    ppermute x1, waiting for transfers between devices: 39.9 us -> 36.9 us  [from_behind(): return lax.ppermute(block, axis, route)]
    concatenate x0 -> x1, other arithmetic: none -> 2.16 us  [gather_by_bits(): jnp.concatenate([line, lax.ppermute(line, axis, [(d, (d - have) % ways) f...]
  transfers between devices with their start and end apart: 3 -> 4, of which waited for: 2 -> 3; matrix products, arithmetic and copies ran while one was open for 13% -> 12% of each run, Pallas kernels for 0% -> 0%
where the time goes in v1:
time: 170 us
  waiting for transfers between devices  66.9 us (39%)
  blocking collectives  45.3 us (27%)
  matrix products  18.3 us (11%)
  between operations  14.1 us (8%)
  other arithmetic  11.3 us (7%)
  starting transfers between devices  7.78 us (5%)
  local copies, waits for them, and re-layouts  6.15 us (4%)
    ppermute x1, waiting for transfers between devices, from_behind(): return lax.ppermute(block, axis, route)  36.9 us
    ppermute x2, waiting for transfers between devices, gather_by_bits(): lax.ppermute(line, axis, [(d, (d - have) % ways) for d in range(ways)])  29.9 us
    psum x1, blocking collectives, on_device(): total_squares = lax.psum(local_squares, 'tensor')  25.2 us
    psum x1, blocking collectives, on_device(): mean_term = lax.psum(local_dot, 'tensor') / D  13.1 us
    dot_general x1, matrix products, on_device(): lax.dot_general(piece, weight, (((1,), (1,)), ((), ())), preferred_elemen...  11.2 us
    dot_general x1, matrix products, on_device(): lax.dot_general(hidden, piece, (((0,), (0,)), ((), ())), preferred_elemen...  7.1 us
    psum x1, blocking collectives, on_device(): gain_total = lax.psum(gain_part, 'dp')  7.03 us
    ppermute x2, starting transfers between devices, gather_by_bits(): lax.ppermute(line, axis, [(d, (d - have) % ways) for d in range(ways)])  6.47 us
  transfers between devices with their start and end apart: 4, of which 3 were waited for; matrix products, arithmetic and copies ran while one was open for 12% of the time, Pallas kernels for 0%

profile of v1, /device:TPU:0, one launch (start us, length us, event | category | flops | bytes accessed | tf_op | source)
XLA Modules:
  0.0 169.8 jit_solution(7563995260880589670)
XLA Ops:
  7.2 0.0 copy-start.1
  7.2 0.0 reduce-scatter.2.cloned.1.call-start
  7.2 5.1 %collective-permute-start = (bf16[512,512]{1,0:T(8,128)(2,1)}, bf16[512,512]{1,0:T(8,128)(2,1)S(1)}, u32[]{:S(2)}, u32[]{:S(2)}) collective-permute-start(bf16[512,512]{1,0:T(8,128)(2,1)} %bitcast.29), channel_id=1, source_target_pairs={{0,3},{1,0},{2,1},{3,2},{4,7},{5,4},{6,5},{7,6},{8,11},{9,8},{10,9... | collective-permute-start | bytes 1572872 | tf_op jit(solution)/shard_map/ppermute | solution.py:14
  12.3 11.5 %collective-permute-done = bf16[512,512]{1,0:T(8,128)(2,1)S(1)} collective-permute-done((bf16[512,512]{1,0:T(8,128)(2,1)}, bf16[512,512]{1,0:T(8,128)(2,1)S(1)}, u32[]{:S(2)}, u32[]{:S(2)}) %collective-permute-start) | collective-permute-done | bytes 524320 | tf_op jit(solution)/shard_map/ppermute | solution.py:14
  23.8 2.2 %pad_maximum_fusion = bf16[512,1024]{1,0:T(8,128)(2,1)} fusion(bf16[512,512]{1,0:T(8,128)(2,1)S(1)} %collective-permute-done, bf16[512,512]{1,0:T(8,128)(2,1)} %bitcast.30), kind=kLoop, calls=%fused_computation.22 | loop fusion | flops 2097152 | bytes 2097152 | tf_op jit(solution)/shard_map/concatenate | solution.py:13
  26.0 1.4 collective-permute-start.1
  27.3 0.7 mul.73
  28.1 2.1 %fusion.13 = f32[512]{0:T(512)S(1)} fusion(bf16[1,1,512,2048]{3,2,1,0:T(8,128)(2,1)} %param.5), kind=kLoop, calls=%fused_computation.16 | loop fusion | flops 3145216 | bytes 2099200 | tf_op jit(solution)/shard_map/reduce_sum | solution.py:34
  30.1 25.2 %psum.21 = f32[512,1]{0,1:T(1,128)S(1)} all-reduce(f32[512,1]{0,1:T(1,128)S(1)} %bitcast.35), channel_id=1, replica_groups=mesh['dp'=4,'pipe'=2,'tensor'=4] {'tensor'}, use_global_device_ids=true, to_apply=%region_1.0 | all-reduce | flops 512 | bytes 4096 | tf_op jit(solution)/shard_map/psum | solution.py:35
  55.3 0.0 copy-done.1
  55.3 0.0 copy-start
  55.3 0.1 constant_dynamic-update-slice_fusion.5
  55.4 0.1 constant_dynamic-update-slice_fusion.4
  55.5 18.5 %collective-permute-done.1 = bf16[512,1024]{1,0:T(8,128)(2,1)} collective-permute-done((bf16[512,1024]{1,0:T(8,128)(2,1)}, bf16[512,1024]{1,0:T(8,128)(2,1)}, u32[]{:S(2)}, u32[]{:S(2)}) %collective-permute-start.1) | collective-permute-done | bytes 1048608 | tf_op jit(solution)/shard_map/ppermute | solution.py:14
  73.9 1.3 constant_dynamic-update-slice_fusion.3
  75.2 0.1 constant_dynamic-update-slice_fusion.2
  75.3 0.1 constant_dynamic-update-slice_fusion.1
  75.4 1.3 constant_dynamic-update-slice_fusion
  76.7 0.0 copy-start.2
  76.7 2.0 %copy-done.2 = bf16[512,4096]{1,0:T(8,128)(2,1)} copy-done((bf16[512,4096]{1,0:T(8,128)(2,1)}, bf16[512,4096]{1,0:T(8,128)(2,1)S(1)}, u32[]{:S(2)}) %copy-start.2) | copy-done | bytes 4194328
  78.7 0.0 copy-done
  78.7 7.1 %convolution_convert_fusion = bf16[2048,2048]{1,0:T(8,128)(2,1)} fusion(bf16[1,1,512,2048]{3,2,1,0:T(8,128)(2,1)S(1)} %copy-done, f32[2048]{0:T(1024)S(1)} %bitcast.32, f32[512]{0:T(512)S(1)} %bitcast.37, bf16[512,4096]{1,0:T(8,128)(2,1)S(1)} %constant_dynamic-update-slice_fusion, s32[]{:T(128)S(6)} %select_n.14), kind=kOutput, calls=%fused_computation.2 | convolution fusion | flops 4303355904 | bytes 12593156 | tf_op jit(solution)/shard_map/dot_general | solution.py:43
  85.8 0.0 reduce-scatter.2.cloned.1.call-update
  85.8 11.2 %fusion.12 = (f32[2048]{0:T(1024)S(1)}, f32[512]{0:T(512)S(1)}, f32[512,2048]{1,0:T(8,128)}) fusion(bf16[1,1,512,2048]{3,2,1,0:T(8,128)(2,1)S(1)} %copy-done, f32[512]{0:T(512)S(1)} %bitcast.38, f32[2048]{0:T(1024)S(1)} %bitcast.33, bf16[1,2048,2048]{2,1,0:T(8,128)(2,1)} %param.9, bf16[512,4096]{1,0:T(8,128)(2,1)} %copy-done.2, s32[]{:T(128)S(6)} %select_n.14), kind=kOutput, calls=%fused_computation.15 | convolution fusion | flops 4302304768 | bytes 16797700 | tf_op jit(solution)/shard_map/dot_general | solution.py:40
  97.0 13.1 %psum.22 = f32[512,1]{0,1:T(1,128)S(1)} all-reduce(f32[512,1]{0,1:T(1,128)S(1)} %bitcast.41), channel_id=1, replica_groups=mesh['dp'=4,'pipe'=2,'tensor'=4] {'tensor'}, use_global_device_ids=true, to_apply=%region_3.4 | all-reduce | flops 512 | bytes 4096 | tf_op jit(solution)/shard_map/psum | solution.py:50
  110.1 6.3 %fusion.10 = bf16[512,2048]{1,0:T(8,128)(2,1)} fusion(f32[512,2048]{1,0:T(8,128)} %get-tuple-element.5, bf16[1,1,512,2048]{3,2,1,0:T(8,128)(2,1)} %param.6, bf16[1,1,512,2048]{3,2,1,0:T(8,128)(2,1)S(1)} %copy-done, f32[512]{0:T(512)S(1)} %bitcast.40, f32[2048]{0:T(1024)S(1)} %bitcast.34, f32[512]{0:T(512)S(1)} %bitcast.39), kind=kLoop, calls=%fused_computation.13 | loop fusion | flops 9437184 | bytes 10498048 | tf_op jit(solution)/shard_map/convert_element_type | solution.py:51
  116.4 1.3 collective-permute-start.2
  117.7 7.0 %psum.23 = f32[1,2048]{1,0:T(1,128)} all-reduce(f32[1,2048]{1,0:T(1,128)S(1)} %bitcast.36), channel_id=1, replica_groups=mesh['dp'=4,'pipe'=2,'tensor'=4] {'dp'}, use_global_device_ids=true, to_apply=%region_6.7 | all-reduce | flops 2048 | bytes 16384 | tf_op jit(solution)/shard_map/psum | solution.py:56
  124.7 36.9 %collective-permute-done.2 = bf16[512,2048]{1,0:T(8,128)(2,1)S(1)} collective-permute-done((bf16[512,2048]{1,0:T(8,128)(2,1)}, bf16[512,2048]{1,0:T(8,128)(2,1)S(1)}, u32[]{:S(2)}, u32[]{:S(2)}) %collective-permute-start.2) | collective-permute-done | bytes 2097184 | tf_op jit(solution)/shard_map/ppermute | solution.py:24
  161.6 0.0 reduce-scatter.2.cloned.1.call-done
  161.6 1.3 copy.14
  (2 shorter events, 0.0 us)
Async XLA Ops:
  7.2 48.2 %copy-start.1 = (bf16[1,1,512,512]{3,2,1,0:T(8,128)(2,1)S(1)}, bf16[1,1,512,512]{3,2,1,0:T(8,128)(2,1)}, u32[]{:S(2)}) copy-start(bf16[1,1,512,512]{3,2,1,0:T(8,128)(2,1)} %param.7) | copy-start | bytes 1572868
  7.2 154.4 %reduce-scatter.2.cloned.1.call-start = ((), (), s32[]{:S(2)}) async-start(), calls=%async_computation.1 | async-start | bytes 10485760 | tf_op jit(solution)/shard_map/reduce_scatter | solution.py:57
  7.2 16.6 %collective-permute-start = (bf16[512,512]{1,0:T(8,128)(2,1)}, bf16[512,512]{1,0:T(8,128)(2,1)S(1)}, u32[]{:S(2)}, u32[]{:S(2)}) collective-permute-start(bf16[512,512]{1,0:T(8,128)(2,1)} %bitcast.29), channel_id=1, source_target_pairs={{0,3},{1,0},{2,1},{3,2},{4,7},{5,4},{6,5},{7,6},{8,11},{9,8},{10,9... | collective-permute-start | bytes 1572872 | tf_op jit(solution)/shard_map/ppermute | solution.py:14
  26.0 47.9 %collective-permute-start.1 = (bf16[512,1024]{1,0:T(8,128)(2,1)}, bf16[512,1024]{1,0:T(8,128)(2,1)}, u32[]{:S(2)}, u32[]{:S(2)}) collective-permute-start(bf16[512,1024]{1,0:T(8,128)(2,1)} %pad_maximum_fusion), channel_id=1, source_target_pairs={{0,2},{1,3},{2,0},{3,1},{4,6},{5,7},{6,4},{7,5},{8,10},{9,11},{10,... | collective-permute-start | bytes 3145736 | tf_op jit(solution)/shard_map/ppermute | solution.py:14
  55.3 23.3 %copy-start = (bf16[1,1,512,2048]{3,2,1,0:T(8,128)(2,1)S(1)}, bf16[1,1,512,2048]{3,2,1,0:T(8,128)(2,1)}, u32[]{:S(2)}) copy-start(bf16[1,1,512,2048]{3,2,1,0:T(8,128)(2,1)} %param.5) | copy-start | bytes 6291460
  76.7 2.0 %copy-start.2 = (bf16[512,4096]{1,0:T(8,128)(2,1)}, bf16[512,4096]{1,0:T(8,128)(2,1)S(1)}, u32[]{:S(2)}) copy-start(bf16[512,4096]{1,0:T(8,128)(2,1)S(1)} %constant_dynamic-update-slice_fusion) | copy-start | bytes 12582916
  116.4 45.2 %collective-permute-start.2 = (bf16[512,2048]{1,0:T(8,128)(2,1)}, bf16[512,2048]{1,0:T(8,128)(2,1)S(1)}, u32[]{:S(2)}, u32[]{:S(2)}) collective-permute-start(bf16[512,2048]{1,0:T(8,128)(2,1)} %fusion.10), channel_id=1, source_target_pairs={{4,0},{5,1},{6,2},{7,3},{12,8},{13,9},{14,10},{15,11},{20,16},{21,... | collective-permute-start | bytes 6291464 | tf_op jit(solution)/shard_map/ppermute | solution.py:24
Sparse Core Ops, SparseCore 0:
  85.9 74.2 reduce-scatter.1
